TPU v7x, 128 devices: a whole 4x4x4 slice. The times are simulated.
128 devices in a mesh: prow: 8 (over x, core), pcol: 16 (over y, z).
Axes of the slice: x: 4, y: 4, z: 4, core: 2. Of those that a mesh axis runs over, the one named last changes fastest.
Arguments:
- basis: bfloat16 [512, 256], replicated, may hold values from -0.25 to 0.25
- potentials: float32 [8, 512], replicated, may hold values from -6 to 6
- orbitals: bfloat16 [64, 512], P('pcol'), may hold values from -6 to 6
- chan_orbital: int32 [256], replicated, may hold values from 0 to 63
- pair_list: int32 [24576, 3], P(('prow', 'pcol')), may hold values from 0 to 255, as said below
- slot_list: int32 [24576], P(('prow', 'pcol')), may hold values from 0 to 255
- coefs: float32 [24576, 2], P(('prow', 'pcol')), may hold values from -6 to 6
- exchange_ops: bfloat16 [24576, 128, 256], P(('prow', 'pcol')), may hold values from -1.1953125 to 1.1953125
Outputs:
- hamiltonian: bfloat16 [32, 8, 2, 16, 256, 256], P(None, 'prow', None, 'pcol')
Inputs may be any that keep to these rules, and one draw needn't show every extreme that they name: `pair_list`: columns 0 and 1 are channels a, b; column 2 is a multipole order below 8. (b // 16 - a // 16) modulo 256 // 16 is below 2. Terms of one device with the same slot s have the same two channels, and the block (a, b) belongs to owner s // 2 in prow-major order: a % 8 and b % 16 are that owner's prow and pcol indices.
All inputs are finite; a program needn't handle non-finite values.
Results may differ from a plain program's by a relative error of at most 0.0058.
Values may be sent and summed in bfloat16 or wider, within the bound.
No kernel may reach another device: no remote copies, remote signals or barrier semaphores. Data moves between devices by JAX's collectives and lax.ppermute only.
A program may use at most 320 MiB of HBM per device.

v0:
```python
import jax
import jax.numpy as jnp
from jax import lax
from jax.sharding import PartitionSpec as P

CAP = 2
BAND = 2
RBLK = 32


def split_bf16(values):
    high = values.astype(jnp.bfloat16)
    low = (values - high.astype(jnp.float32)).astype(jnp.bfloat16)
    return (high, low)


def on_device(basis, potentials, orbitals, chan_orbital, pair_list, slot_list, coefs, exchange_ops):
    all_orbitals = lax.all_gather(orbitals, "pcol", axis=0, tiled=True)
    row_devs = lax.axis_size("prow")
    col_devs = lax.axis_size("pcol")
    slot_count = row_devs * col_devs * CAP
    chan_count = chan_orbital.shape[0]
    orb_count = all_orbitals.shape[0]
    point_count = basis.shape[0]
    spline_count = basis.shape[1]
    inner_count = exchange_ops.shape[1]
    term_count = exchange_ops.shape[0]
    col_groups = chan_count // col_devs
    block_count = RBLK * BAND
    first_chan = pair_list[:, 0]
    second_chan = pair_list[:, 1]
    multipole = pair_list[:, 2]
    channels = jnp.arange(chan_count, dtype=jnp.int32)
    orb_ids = jnp.arange(orb_count, dtype=jnp.int32)
    first_orb = jnp.sum(
        jnp.where(first_chan[:, None] == channels[None, :], chan_orbital[None, :], 0), axis=1
    )
    second_orb = jnp.sum(
        jnp.where(second_chan[:, None] == channels[None, :], chan_orbital[None, :], 0), axis=1
    )
    first_rows = jnp.dot(
        (first_orb[:, None] == orb_ids[None, :]).astype(jnp.bfloat16),
        all_orbitals,
        preferred_element_type=jnp.float32,
    )
    second_rows = jnp.dot(
        (second_orb[:, None] == orb_ids[None, :]).astype(jnp.bfloat16),
        all_orbitals,
        preferred_element_type=jnp.float32,
    )
    pick_pot = (
        multipole[:, None] == jnp.arange(potentials.shape[0], dtype=jnp.int32)[None, :]
    ).astype(jnp.float32)
    pot_rows = jnp.dot(pick_pot, potentials, precision=lax.Precision.HIGHEST)
    radial = coefs[:, 0:1] * pot_rows + coefs[:, 1:2] * (first_rows * second_rows)
    matches = slot_list[None, :] == jnp.arange(slot_count, dtype=jnp.int32)[:, None]
    slot_weight = jnp.dot(
        matches.astype(jnp.float32), radial, precision=lax.Precision.HIGHEST
    ).astype(jnp.bfloat16)
    exchange_rows = exchange_ops.reshape(term_count, inner_count * spline_count)
    slot_exchange = jnp.dot(
        matches.astype(jnp.bfloat16), exchange_rows, preferred_element_type=jnp.float32
    ).astype(jnp.bfloat16)
    offset = jnp.mod(second_chan // col_devs - first_chan // col_devs, col_groups)
    block_index = first_chan // row_devs * BAND + offset
    slot_ids = jnp.max(jnp.where(matches, block_index[None, :], -1), axis=1)
    payload = inner_count * spline_count + point_count + 1
    width = -(-payload // 128) * 128
    packed = jnp.concatenate(
        [
            slot_exchange,
            slot_weight,
            slot_ids.astype(jnp.bfloat16)[:, None],
            jnp.zeros((slot_count, width - payload), jnp.bfloat16),
        ],
        axis=1,
    )
    received = lax.all_to_all(packed, ("prow", "pcol"), 0, 0, tiled=True)
    idents = received[:, payload - 1].astype(jnp.float32).astype(jnp.int32)
    select = (jnp.arange(block_count, dtype=jnp.int32)[:, None] == idents[None, :]).astype(
        jnp.bfloat16
    )
    summed = jnp.dot(select, received[:, : payload - 1], preferred_element_type=jnp.float32)
    exchange_sum = summed[:, : inner_count * spline_count].reshape(
        block_count, inner_count, spline_count
    )
    weight_sum = summed[:, inner_count * spline_count :]
    basis_float = basis.astype(jnp.float32)
    scaled_high, scaled_low = split_bf16(weight_sum[:, :, None] * basis_float[None])
    exchange_high, exchange_low = split_bf16(exchange_sum)
    inner_rows = basis[:inner_count]
    tiles = (
        jnp.einsum("qa,gqb->gab", basis, scaled_high, preferred_element_type=jnp.float32)
        + jnp.einsum("qa,gqb->gab", basis, scaled_low, preferred_element_type=jnp.float32)
        + jnp.einsum("qa,gqb->gab", inner_rows, exchange_high, preferred_element_type=jnp.float32)
        + jnp.einsum("qa,gqb->gab", inner_rows, exchange_low, preferred_element_type=jnp.float32)
    )
    return tiles.astype(jnp.bfloat16).reshape(RBLK, 1, BAND, 1, spline_count, spline_count)


def solution(mesh):
    placed = (
        P(),
        P(),
        P("pcol", None),
        P(),
        P(("prow", "pcol"), None),
        P(("prow", "pcol")),
        P(("prow", "pcol"), None),
        P(("prow", "pcol"), None, None),
    )
    return jax.shard_map(
        on_device,
        mesh=mesh,
        in_specs=placed,
        out_specs=P(None, "prow", None, "pcol", None, None),
        check_vma=False,
    )
```

profile of v0, /device:TPU:23, one launch (start us, length us, event | category | flops | bytes accessed | tf_op | source)
XLA Modules:
  0.0 489.6 jit_solution(6347302952289938058)
XLA Ops:
  0.0 0.8 fusion.31
  0.8 0.8 fusion.30
  1.6 0.8 select_reduce_fusion
  2.4 0.9 select_reduce_fusion.1
  3.3 0.2 convert_element_type.87
  3.6 18.1 %all-gather = bf16[16,4,512]{2,1,0:T(4,128)(2,1)S(1)} all-gather(bf16[1,4,512]{2,1,0:T(4,128)(2,1)} %bitcast.40), channel_id=1, replica_groups=mesh['prow'=8,'pcol'=16] {'pcol'}, dimensions={0}, use_global_device_ids=true | all-gather | bytes 69632 | tf_op jit(solution)/shard_map/all_gather | solution.py:18
  21.7 0.2 fusion.19
  22.0 0.3 fusion.14
  22.3 0.4 fusion.13
  22.6 1.2 convolution_convert_fusion.1
  23.8 0.1 concatenate.9
  23.9 13.9 %copy.34 = bf16[24,8,128,256]{3,1,2,0:T(8,128)(2,1)} copy(bf16[24,8,128,256]{3,2,1,0:T(8,128)(2,1)} %bitcast.32) | data formatting | bytes 25165824
  37.8 12.7 %convolution_convert_fusion = bf16[256,32768]{1,0:T(8,128)(2,1)} fusion(bf16[192,32768]{1,0:T(8,128)(2,1)} %bitcast.28, s32[192]{0:T(256)S(1)} %copy-done.4), kind=kOutput, calls=%fused_computation.2 | convolution fusion | flops 3229663232 | bytes 29360896 | tf_op jit(solution)/shard_map/dot_general | solution.py:61
  50.6 27.1 %concatenate.8 = bf16[128,2,32768]{2,1,0:T(2,128)(2,1)} reshape(bf16[256,32768]{1,0:T(8,128)(2,1)} %convolution_convert_fusion) | data formatting | bytes 33554432 | tf_op jit(solution)/shard_map/concatenate | solution.py:69
  77.6 14.1 %constant_dynamic-update-slice_fusion.1 = bf16[128,2,33408]{2,1,0:T(2,128)(2,1)} fusion(bf16[128,2,32768]{2,1,0:T(2,128)(2,1)} %concatenate.8), kind=kLoop, calls=%fused_computation.47 | loop fusion | bytes 33554432
  91.8 0.9 constant_dynamic-update-slice_fusion
  92.7 3.3 dynamic-update-slice.2
  96.0 21.9 %dynamic-update-slice.3 = bf16[128,2,33408]{2,1,0:T(2,128)(2,1)} dynamic-update-slice(bf16[128,2,33408]{2,1,0:T(2,128)(2,1)} %dynamic-update-slice.2, bf16[128,2,127]{2,1,0:T(2,128)(2,1)S(1)} %broadcast_in_dim.52, s32[]{} %constant.60, s32[]{} %constant.60, s32[]{} %constant.63) | dynamic-update-slice | bytes 130052 | tf_op jit(solution)/shard_map/concatenate | solution.py:69
  117.9 14.7 %all-to-all-start = ((bf16[128,2,33408]{2,1,0:T(2,128)(2,1)}), bf16[128,2,33408]{2,1,0:T(2,128)(2,1)}, u32[]{:S(2)}, u32[]{:S(2)}) async-start(bf16[128,2,33408]{2,1,0:T(2,128)(2,1)} %dynamic-update-slice.3), calls=%async_computation | async-start | bytes 34209792 | tf_op jit(solution)/shard_map/all_to_all | solution.py:78
  132.6 0.1 copy.30
  132.8 239.9 %all-to-all-done = bf16[128,2,33408]{2,1,0:T(2,128)(2,1)} async-done(((bf16[128,2,33408]{2,1,0:T(2,128)(2,1)}), bf16[128,2,33408]{2,1,0:T(2,128)(2,1)}, u32[]{:S(2)}, u32[]{:S(2)}) %all-to-all-start) | async-done | bytes 17104928 | tf_op jit(solution)/shard_map/all_to_all | solution.py:78
  372.7 25.3 %all_to_all.7 = bf16[256,33408]{1,0:T(8,128)(2,1)} reshape(bf16[128,2,33408]{2,1,0:T(2,128)(2,1)} %all-to-all-done) | data formatting | bytes 34209792 | tf_op jit(solution)/shard_map/all_to_all | solution.py:78
  398.1 1.0 convert_reduce_fusion
  399.0 7.5 %fusion.2 = f32[64,33280]{1,0:T(8,128)S(1)} fusion(bf16[256,33408]{1,0:T(8,128)(2,1)} %all_to_all.7, s32[256]{0:T(256)S(1)} %convert_reduce_fusion), kind=kOutput, calls=%fused_computation.5 | convolution fusion | flops 1090535424 | bytes 25560064 | tf_op jit(solution)/shard_map/dot_general | solution.py:83
  406.5 3.9 slice.43
  410.5 8.0 %fusion.4 = f32[64,256,256]{2,1,0:T(8,128)} fusion(f32[512,256]{0,1:T(8,128)S(1)} %copy.30, f32[64,512]{1,0:T(8,128)S(1)} %slice.42, bf16[512,256]{1,0:T(8,128)(2,1)S(1)} %copy-done.3), kind=kOutput, calls=%fused_computation.7 | convolution fusion | flops 4336910336 | bytes 17694720 | tf_op jit(solution)/shard_map/qa,gqb->gab/dot_general | solution.py:94
  418.5 8.0 %fusion.1 = f32[64,256,256]{2,1,0:T(8,128)} fusion(f32[512,256]{0,1:T(8,128)S(1)} %copy.30, f32[64,512]{1,0:T(8,128)S(1)} %slice.42, bf16[512,256]{1,0:T(8,128)(2,1)S(1)} %copy-done.3), kind=kOutput, calls=%fused_computation.4 | convolution fusion | flops 4311744512 | bytes 17694720 | tf_op jit(solution)/shard_map/qa,gqb->gab/dot_general | solution.py:93
  426.5 5.9 %copy.35 = f32[8,8,128,256]{3,2,1,0:T(8,128)} copy(f32[8,8,128,256]{3,1,2,0:T(8,128)S(1)} %bitcast.30) | data formatting | bytes 16777216
  432.4 9.0 %copy.31 = f32[64,128,256]{1,2,0:T(8,128)} copy(f32[64,128,256]{2,1,0:T(8,128)} %bitcast.31) | data formatting | bytes 16777216 | tf_op jit(solution)/shard_map/reshape | solution.py:84
  441.4 11.4 %fusion.11 = f32[64,256,256]{2,1,0:T(8,128)} fusion(f32[64,128,256]{1,2,0:T(8,128)} %copy.31, bf16[512,256]{1,0:T(8,128)(2,1)S(1)} %copy-done.3), kind=kOutput, calls=%fused_computation.15 | convolution fusion | flops 1075838976 | bytes 25231360 | tf_op jit(solution)/shard_map/qa,gqb->gab/dot_general | solution.py:95
  452.8 24.9 %add_convert_fusion = bf16[64,256,256]{2,1,0:T(8,128)(2,1)} fusion(f32[64,256,256]{2,1,0:T(8,128)} %fusion.11, f32[64,256,256]{2,1,0:T(8,128)} %fusion.1, f32[64,256,256]{2,1,0:T(8,128)} %fusion.4, f32[64,128,256]{1,2,0:T(8,128)} %copy.31, bf16[512,256]{1,0:T(8,128)(2,1)S(1)} %copy-done.3), kind=kOutput, calls=%fused_computation.8 | convolution fusion | flops 1098907648 | bytes 67174400 | tf_op jit(solution)/shard_map/qa,gqb->gab/dot_general | solution.py:96
  477.7 11.9 %copy.33 = bf16[32,1,2,1,256,256]{5,4,3,2,1,0:T(8,128)(2,1)} copy(bf16[32,1,2,1,256,256]{4,5,2,0,3,1:T(8,128)(2,1)} %bitcast.29) | data formatting | bytes 16777216 | tf_op jit(solution)/shard_map/reshape | solution.py:98
  (15 shorter events, 0.1 us)
Async XLA Ops:
  0.0 22.3 %copy-start = (f32[8,512]{1,0:T(8,128)S(1)}, f32[8,512]{1,0:T(8,128)}, u32[]{:S(2)}) copy-start(f32[8,512]{1,0:T(8,128)} %param.9) | copy-start | bytes 49156
  0.0 37.8 %copy-start.4 = (s32[192]{0:T(256)S(1)}, s32[192]{0:T(256)}, u32[]{:S(2)}) copy-start(s32[192]{0:T(256)} %param.13) | copy-start | bytes 2308
  117.9 14.8 %copy-start.3 = (bf16[512,256]{1,0:T(8,128)(2,1)S(1)}, bf16[512,256]{1,0:T(8,128)(2,1)}, u32[]{:S(2)}) copy-start(bf16[512,256]{1,0:T(8,128)(2,1)} %param.8) | copy-start | bytes 786436
  117.9 254.8 %all-to-all-start = ((bf16[128,2,33408]{2,1,0:T(2,128)(2,1)}), bf16[128,2,33408]{2,1,0:T(2,128)(2,1)}, u32[]{:S(2)}, u32[]{:S(2)}) async-start(bf16[128,2,33408]{2,1,0:T(2,128)(2,1)} %dynamic-update-slice.3), calls=%async_computation | async-start | bytes 34209792 | tf_op jit(solution)/shard_map/all_to_all | solution.py:78
  418.5 8.0 %copy-start.2 = (f32[64,32768]{1,0:T(8,128)S(1)}, f32[64,32768]{1,0:T(8,128)}, u32[]{:S(2)}) copy-start(f32[64,32768]{1,0:T(8,128)} %slice.43) | copy-start | bytes 25165828
  452.8 36.8 %copy-start.1 = (f32[8,512]{1,0:T(8,128)S(1)}, f32[8,512]{1,0:T(8,128)}, u32[]{:S(2)}) copy-start(f32[8,512]{1,0:T(8,128)} %param.9) | copy-start | bytes 49156
where the time goes:
time: 492 us; the launch traced here: 490 us
  waiting for transfers between devices  240 us (49%)
  local copies, waits for them, and re-layouts  139 us (28%)
  matrix products  74.7 us (15%)
  blocking collectives  18.1 us (4%)
  starting transfers between devices  14.7 us (3%)
    all_to_all x1, waiting for transfers between devices, on_device(): received = lax.all_to_all(packed, ('prow', 'pcol'), 0, 0, tiled=True)  240 us
    concatenate x3, local copies, waits for them, and re-layouts, on_device(): jnp.concatenate([slot_exchange, slot_weight, slot_ids.astype(jnp.bfloat16...  49.1 us
    unnamed x16, local copies, waits for them, and re-layouts  38.1 us
    all_to_all x1, local copies, waits for them, and re-layouts, on_device(): received = lax.all_to_all(packed, ('prow', 'pcol'), 0, 0, tiled=True)  25.3 us
    dot_general x1, matrix products, on_device(): jnp.einsum('qa,gqb->gab', inner_rows, exchange_low, preferred_element_typ...  24.9 us
    all_gather x1, blocking collectives, on_device(): all_orbitals = lax.all_gather(orbitals, 'pcol', axis=0, tiled=True)  18.1 us
    all_to_all x1, starting transfers between devices, on_device(): received = lax.all_to_all(packed, ('prow', 'pcol'), 0, 0, tiled=True)  14.7 us
    dot_general x1, matrix products, on_device(): jnp.dot(matches.astype(jnp.bfloat16), exchange_rows, preferred_element_ty...  12.7 us
  transfers between devices with their start and end apart: 1, of which 1 were waited for; matrix products, arithmetic and copies ran while one was open for 0% of the time, Pallas kernels for 0%

commit v1 on v0

--- a/solution.py
+++ b/solution.py
@@ -15,7 +15,16 @@
 
 
 def on_device(basis, potentials, orbitals, chan_orbital, pair_list, slot_list, coefs, exchange_ops):
-    all_orbitals = lax.all_gather(orbitals, "pcol", axis=0, tiled=True)
+    ways = lax.axis_size("pcol")
+    up = [(d, (d + 1) % ways) for d in range(ways)]
+    down = [(d, (d - 1) % ways) for d in range(ways)]
+    earlier, later = ([orbitals], [orbitals])
+    for _ in range(ways // 2):
+        earlier.append(lax.ppermute(earlier[-1], "pcol", up))
+    for _ in range((ways - 1) // 2):
+        later.append(lax.ppermute(later[-1], "pcol", down))
+    line = jnp.concatenate([*earlier[::-1], *later[1:]], axis=0)
+    all_orbitals = jnp.roll(line, (lax.axis_index("pcol") - ways // 2) * orbitals.shape[0], axis=0)
     row_devs = lax.axis_size("prow")
     col_devs = lax.axis_size("pcol")
     slot_count = row_devs * col_devs * CAP

time: 492 us -> 515 us (1.047)
  starting transfers between devices: 14.7 us -> 50.7 us
  blocking collectives: 18.1 us -> 0 us
  waiting for transfers between devices: 240 us -> 248 us
    ppermute x0 -> x15, starting transfers between devices: none -> 26.5 us  [the longest x7 24.8 us: on_device(): later.append(lax.ppermute(later[-1], 'pcol', down))]
    all_gather x1 -> x0, blocking collectives: 18.1 us -> none  [on_device(): all_orbitals = lax.all_gather(orbitals, 'pcol', axis=0, tiled=True)]
    all_to_all x1, starting transfers between devices: 14.7 us -> 24.2 us  [on_device(): received = lax.all_to_all(packed, ('prow', 'pcol'), 0, 0, tiled=True)]
    ppermute x0 -> x15, waiting for transfers between devices: none -> 7.38 us  [the longest x8 4.24 us: on_device(): earlier.append(lax.ppermute(earlier[-1], 'pcol', up))]
    unnamed x16 -> x23, local copies, waits for them, and re-layouts: 38.1 us -> 38.2 us
  transfers between devices with their start and end apart: 1 -> 16, of which waited for: 1 -> 10; matrix products, arithmetic and copies ran while one was open for 0% -> 13% of each run, Pallas kernels for 0% -> 0%
where the time goes in v1:
time: 515 us; the launch traced here: 513 us
  waiting for transfers between devices  248 us (48%)
  local copies, waits for them, and re-layouts  138 us (27%)
  matrix products  74.1 us (14%)
  starting transfers between devices  50.7 us (10%)
    all_to_all x1, waiting for transfers between devices, on_device(): received = lax.all_to_all(packed, ('prow', 'pcol'), 0, 0, tiled=True)  241 us
    concatenate x3, local copies, waits for them, and re-layouts, on_device(): jnp.concatenate([slot_exchange, slot_weight, slot_ids.astype(jnp.bfloat16...  49 us
    unnamed x23, local copies, waits for them, and re-layouts  38.2 us
    all_to_all x1, local copies, waits for them, and re-layouts, on_device(): received = lax.all_to_all(packed, ('prow', 'pcol'), 0, 0, tiled=True)  25.3 us
    dot_general x1, matrix products, on_device(): jnp.einsum('qa,gqb->gab', inner_rows, exchange_low, preferred_element_typ...  25 us
    ppermute x7, starting transfers between devices, on_device(): later.append(lax.ppermute(later[-1], 'pcol', down))  24.8 us
    all_to_all x1, starting transfers between devices, on_device(): received = lax.all_to_all(packed, ('prow', 'pcol'), 0, 0, tiled=True)  24.2 us
    dot_general x1, matrix products, on_device(): jnp.dot(matches.astype(jnp.bfloat16), exchange_rows, preferred_element_ty...  12.8 us
  transfers between devices with their start and end apart: 16, of which 10 were waited for; matrix products, arithmetic and copies ran while one was open for 13% of the time, Pallas kernels for 0%

profile of v1, /device:TPU:23, one launch (start us, length us, event | category | flops | bytes accessed | tf_op | source)
XLA Modules:
  0.0 512.9 jit_solution(13247662020091904132)
XLA Ops:
  0.0 1.6 collective-permute-start
  1.6 2.1 collective-permute-start.8
  3.7 13.9 %copy.29 = bf16[24,8,128,256]{3,1,2,0:T(8,128)(2,1)} copy(bf16[24,8,128,256]{3,2,1,0:T(8,128)(2,1)} %bitcast.29) | data formatting | bytes 25165824
  17.7 12.8 %convolution_convert_fusion = bf16[256,32768]{1,0:T(8,128)(2,1)} fusion(bf16[192,32768]{1,0:T(8,128)(2,1)} %bitcast.25, s32[192]{0:T(256)S(1)} %copy-done.4), kind=kOutput, calls=%fused_computation.2 | convolution fusion | flops 3229663232 | bytes 29360896 | tf_op jit(solution)/shard_map/dot_general | solution.py:70
  30.5 27.0 %concatenate.14 = bf16[128,2,32768]{2,1,0:T(2,128)(2,1)} reshape(bf16[256,32768]{1,0:T(8,128)(2,1)} %convolution_convert_fusion) | data formatting | bytes 33554432 | tf_op jit(solution)/shard_map/concatenate | solution.py:78
  57.5 14.1 %constant_dynamic-update-slice_fusion.1 = bf16[128,2,33408]{2,1,0:T(2,128)(2,1)} fusion(bf16[128,2,32768]{2,1,0:T(2,128)(2,1)} %concatenate.14), kind=kLoop, calls=%fused_computation.49 | loop fusion | bytes 33554432
  71.6 3.6 collective-permute-start.9
  75.3 0.7 collective-permute-done.9
  76.0 3.8 collective-permute-start.10
  79.9 0.7 collective-permute-done.10
  80.6 3.8 collective-permute-start.11
  85.2 3.8 collective-permute-start.12
  89.0 0.7 collective-permute-done.12
  89.7 3.8 collective-permute-start.13
  94.3 3.8 collective-permute-start.14
  98.9 4.0 collective-permute-done.7
  104.4 0.9 constant_dynamic-update-slice_fusion
  105.3 3.3 dynamic-update-slice.2
  108.6 21.9 %dynamic-update-slice.3 = bf16[128,2,33408]{2,1,0:T(2,128)(2,1)} dynamic-update-slice(bf16[128,2,33408]{2,1,0:T(2,128)(2,1)} %dynamic-update-slice.2, bf16[128,2,127]{2,1,0:T(2,128)(2,1)S(1)} %broadcast_in_dim.52, s32[]{} %constant.88, s32[]{} %constant.88, s32[]{} %constant.91) | dynamic-update-slice | bytes 130052 | tf_op jit(solution)/shard_map/concatenate | solution.py:78
  130.6 24.2 %all-to-all-start = ((bf16[128,2,33408]{2,1,0:T(2,128)(2,1)}), bf16[128,2,33408]{2,1,0:T(2,128)(2,1)}, u32[]{:S(2)}, u32[]{:S(2)}) async-start(bf16[128,2,33408]{2,1,0:T(2,128)(2,1)} %dynamic-update-slice.3), calls=%async_computation | async-start | bytes 34209792 | tf_op jit(solution)/shard_map/all_to_all | solution.py:87
  155.0 241.0 %all-to-all-done = bf16[128,2,33408]{2,1,0:T(2,128)(2,1)} async-done(((bf16[128,2,33408]{2,1,0:T(2,128)(2,1)}), bf16[128,2,33408]{2,1,0:T(2,128)(2,1)}, u32[]{:S(2)}, u32[]{:S(2)}) %all-to-all-start) | async-done | bytes 17104928 | tf_op jit(solution)/shard_map/all_to_all | solution.py:87
  395.9 25.3 %all_to_all.7 = bf16[256,33408]{1,0:T(8,128)(2,1)} reshape(bf16[128,2,33408]{2,1,0:T(2,128)(2,1)} %all-to-all-done) | data formatting | bytes 34209792 | tf_op jit(solution)/shard_map/all_to_all | solution.py:87
  421.2 1.0 convert_reduce_fusion
  422.1 7.5 %fusion.2 = f32[64,33280]{1,0:T(8,128)S(1)} fusion(bf16[256,33408]{1,0:T(8,128)(2,1)} %all_to_all.7, s32[256]{0:T(256)S(1)} %convert_reduce_fusion), kind=kOutput, calls=%fused_computation.5 | convolution fusion | flops 1090535424 | bytes 25560064 | tf_op jit(solution)/shard_map/dot_general | solution.py:92
  429.6 3.9 slice.43
  433.6 8.1 %fusion.4 = f32[64,256,256]{2,1,0:T(8,128)} fusion(f32[512,256]{0,1:T(8,128)S(1)} %copy.25, f32[64,512]{1,0:T(8,128)S(1)} %slice.42, bf16[512,256]{1,0:T(8,128)(2,1)S(1)} %copy-done.3), kind=kOutput, calls=%fused_computation.7 | convolution fusion | flops 4336910336 | bytes 17694720 | tf_op jit(solution)/shard_map/qa,gqb->gab/dot_general | solution.py:103
  441.6 8.0 %fusion.1 = f32[64,256,256]{2,1,0:T(8,128)} fusion(f32[512,256]{0,1:T(8,128)S(1)} %copy.25, f32[64,512]{1,0:T(8,128)S(1)} %slice.42, bf16[512,256]{1,0:T(8,128)(2,1)S(1)} %copy-done.3), kind=kOutput, calls=%fused_computation.4 | convolution fusion | flops 4311744512 | bytes 17694720 | tf_op jit(solution)/shard_map/qa,gqb->gab/dot_general | solution.py:102
  449.7 5.9 %copy.30 = f32[8,8,128,256]{3,2,1,0:T(8,128)} copy(f32[8,8,128,256]{3,1,2,0:T(8,128)S(1)} %bitcast.27) | data formatting | bytes 16777216
  455.6 9.0 %copy.26 = f32[64,128,256]{1,2,0:T(8,128)} copy(f32[64,128,256]{2,1,0:T(8,128)} %bitcast.28) | data formatting | bytes 16777216 | tf_op jit(solution)/shard_map/reshape | solution.py:93
  464.6 11.5 %fusion.11 = f32[64,256,256]{2,1,0:T(8,128)} fusion(f32[64,128,256]{1,2,0:T(8,128)} %copy.26, bf16[512,256]{1,0:T(8,128)(2,1)S(1)} %copy-done.3), kind=kOutput, calls=%fused_computation.15 | convolution fusion | flops 1075838976 | bytes 25231360 | tf_op jit(solution)/shard_map/qa,gqb->gab/dot_general | solution.py:104
  476.0 25.0 %add_convert_fusion = bf16[64,256,256]{2,1,0:T(8,128)(2,1)} fusion(f32[64,256,256]{2,1,0:T(8,128)} %fusion.11, f32[64,256,256]{2,1,0:T(8,128)} %fusion.1, f32[64,256,256]{2,1,0:T(8,128)} %fusion.4, f32[64,128,256]{1,2,0:T(8,128)} %copy.26, bf16[512,256]{1,0:T(8,128)(2,1)S(1)} %copy-done.3), kind=kOutput, calls=%fused_computation.8 | convolution fusion | flops 1098907648 | bytes 67174400 | tf_op jit(solution)/shard_map/qa,gqb->gab/dot_general | solution.py:105
  501.0 11.9 %copy.28 = bf16[32,1,2,1,256,256]{5,4,3,2,1,0:T(8,128)(2,1)} copy(bf16[32,1,2,1,256,256]{4,5,2,0,3,1:T(8,128)(2,1)} %bitcast.26) | data formatting | bytes 16777216 | tf_op jit(solution)/shard_map/reshape | solution.py:107
  (52 shorter events, 4.1 us)
Async XLA Ops:
  0.0 84.4 %copy-start = (f32[8,512]{1,0:T(8,128)S(1)}, f32[8,512]{1,0:T(8,128)}, u32[]{:S(2)}) copy-start(f32[8,512]{1,0:T(8,128)} %param.9) | copy-start | bytes 49156
  0.0 17.7 %copy-start.4 = (s32[192]{0:T(256)S(1)}, s32[192]{0:T(256)}, u32[]{:S(2)}) copy-start(s32[192]{0:T(256)} %param.13) | copy-start | bytes 2308
  0.0 57.4 %collective-permute-start = (bf16[4,512]{1,0:T(4,128)(2,1)}, bf16[4,512]{1,0:T(4,128)(2,1)S(1)}, u32[]{:S(2)}, u32[]{:S(2)}) collective-permute-start(bf16[4,512]{1,0:T(4,128)(2,1)} %param.10), channel_id=1, source_target_pairs={{0,1},{1,2},{2,3},{3,4},{4,5},{5,6},{6,7},{7,8},{8,9},{9,10},{10,1... | collective-permute-start | bytes 12296 | tf_op jit(solution)/shard_map/ppermute | solution.py:23
  1.6 70.0 %collective-permute-start.8 = (bf16[4,512]{1,0:T(4,128)(2,1)}, bf16[4,512]{1,0:T(4,128)(2,1)S(1)}, u32[]{:S(2)}, u32[]{:S(2)}) collective-permute-start(bf16[4,512]{1,0:T(4,128)(2,1)} %param.10), channel_id=1, source_target_pairs={{0,15},{1,0},{2,1},{3,2},{4,3},{5,4},{6,5},{7,6},{8,7},{9,8},{10,9... | collective-permute-start | bytes 12296 | tf_op jit(solution)/shard_map/ppermute | solution.py:25
  57.4 17.9 %copy-start.6 = (s32[192,3]{0,1:T(4,128)S(1)}, s32[192,3]{0,1:T(4,128)}, u32[]{:S(2)}) copy-start(s32[192,3]{0,1:T(4,128)} %param.12) | copy-start | bytes 6916
  57.4 22.4 %copy-start.7 = (f32[192,2]{0,1:T(2,128)S(1)}, f32[192,2]{0,1:T(2,128)}, u32[]{:S(2)}) copy-start(f32[192,2]{0,1:T(2,128)} %param.14) | copy-start | bytes 4612
  57.4 36.3 %copy-start.8 = (s32[256]{0:T(256)S(1)}, s32[256]{0:T(256)}, u32[]{:S(2)}) copy-start(s32[256]{0:T(256)} %param.11) | copy-start | bytes 3076
  57.4 45.4 %copy-start.5 = (bf16[4,512]{1,0:T(4,128)(2,1)S(1)}, bf16[4,512]{1,0:T(4,128)(2,1)}, u32[]{:S(2)}) copy-start(bf16[4,512]{1,0:T(4,128)(2,1)} %param.10) | copy-start | bytes 12292
  57.4 17.8 %collective-permute-start.1 = (bf16[4,512]{1,0:T(4,128)(2,1)S(1)}, bf16[4,512]{1,0:T(4,128)(2,1)S(1)}, u32[]{:S(2)}, u32[]{:S(2)}) collective-permute-start(bf16[4,512]{1,0:T(4,128)(2,1)S(1)} %collective-permute-done), channel_id=1, source_target_pairs={{0,1},{1,2},{2,3},{3,4},{4,5},{5,6},{6,7},{7,8},{8,9},{9,10},{10,1... | collective-permute-start | bytes 12296 | tf_op jit(solution)/shard_map/ppermute | solution.py:23
  71.6 4.4 collective-permute-start.9
  75.3 4.6 collective-permute-start.2
  76.0 4.6 collective-permute-start.10
  79.8 4.6 collective-permute-start.3
  80.6 4.6 collective-permute-start.11
  84.4 4.6 collective-permute-start.4
  85.2 4.6 collective-permute-start.12
  89.0 4.7 collective-permute-start.5
  89.7 4.6 collective-permute-start.13
  93.7 4.6 collective-permute-start.6
  94.3 4.6 collective-permute-start.14
  98.2 4.6 collective-permute-start.7
  130.6 24.2 %copy-start.3 = (bf16[512,256]{1,0:T(8,128)(2,1)S(1)}, bf16[512,256]{1,0:T(8,128)(2,1)}, u32[]{:S(2)}) copy-start(bf16[512,256]{1,0:T(8,128)(2,1)} %param.8) | copy-start | bytes 786436
  130.6 265.4 %all-to-all-start = ((bf16[128,2,33408]{2,1,0:T(2,128)(2,1)}), bf16[128,2,33408]{2,1,0:T(2,128)(2,1)}, u32[]{:S(2)}, u32[]{:S(2)}) async-start(bf16[128,2,33408]{2,1,0:T(2,128)(2,1)} %dynamic-update-slice.3), calls=%async_computation | async-start | bytes 34209792 | tf_op jit(solution)/shard_map/all_to_all | solution.py:87
  441.6 8.0 %copy-start.2 = (f32[64,32768]{1,0:T(8,128)S(1)}, f32[64,32768]{1,0:T(8,128)}, u32[]{:S(2)}) copy-start(f32[64,32768]{1,0:T(8,128)} %slice.43) | copy-start | bytes 25165828
  476.0 36.9 %copy-start.1 = (f32[8,512]{1,0:T(8,128)S(1)}, f32[8,512]{1,0:T(8,128)}, u32[]{:S(2)}) copy-start(f32[8,512]{1,0:T(8,128)} %param.9) | copy-start | bytes 49156
